TPU v7x, 32 devices: a whole 2x2x4 slice. The times are simulated.
32 devices in a mesh: tm: 16 (over z, x, core), doc: 2 (over y).
Axes of the slice: x: 2, y: 2, z: 4, core: 2. Of those that a mesh axis runs over, the one named last changes fastest.
Arguments:
- beta: float32 [16, 4096, 128], P('tm', 'doc'), may hold values from -6 to 260
- word_ids: int32 [16, 8, 128], P('tm', 'doc'), may hold values from 0 to 4095
- word_counts: int32 [16, 8, 128], P('tm', 'doc'), may hold values from 1 to 8
- block_slot: int32 [32], replicated, may hold values from 0 to 31, each once
- topic_prior: float32 [128], replicated, may hold values from 0.05 to 0.5
- drift_var: float32 [128], replicated, may hold values from 0.0005 to 0.05
- obs_precision: float32 [16, 128], replicated, may hold values from 0.01 to 4
Outputs:
- smoothed_means: float32 [16, 4096, 128], P('tm', 'doc')
- doc_topics: float32 [16, 8, 128], P('tm', 'doc')
Inputs may be any that keep to these rules, and one draw needn't show every extreme that they name: `block_slot`: each block has its own position.
All inputs are finite; a program needn't handle non-finite values.
Results may differ from a plain program's by a relative error of at most 0.0012.
The roundings to bfloat16 on the way count: a program that leaves them out, or rounds other values in their place, can miss the bound.
Values may be sent and summed in bfloat16 or wider, within the bound.
No kernel may reach another device: no remote copies, remote signals or barrier semaphores. Data moves between devices by JAX's collectives and lax.ppermute only.
A program may use at most 192 MiB of HBM per device.

v0:
```python
import jax
import jax.numpy as jnp
from jax import lax
from jax.sharding import PartitionSpec as P

K = 128
BLOCK = 128
EITERS = 4
init_variance = 4.0


def variance_tables(obs_precision, drift_var):

    def forward_step(prior_var, precision):
        denominator = 1.0 + prior_var * precision
        gain_now = prior_var * precision / denominator
        filt_var = prior_var / denominator
        return (filt_var + drift_var, (gain_now, filt_var))

    start_var = jnp.full(drift_var.shape, init_variance, dtype=jnp.float32)
    last_var, (gains, filt_vars) = lax.scan(forward_step, start_var, obs_precision)

    def backward_step(info_next, precision):
        merged = info_next + precision
        shrink = 1.0 / (1.0 + drift_var * merged)
        info_now = merged * shrink
        return (info_now, (shrink, info_now))

    zero_info = jnp.zeros(drift_var.shape, dtype=jnp.float32)
    last_info, (shrinks, infos) = lax.scan(
        backward_step, zero_info, obs_precision[1:], reverse=True
    )
    shrinks = jnp.concatenate([shrinks, jnp.ones_like(zero_info)[None]], axis=0)
    infos = jnp.concatenate([infos, zero_info[None]], axis=0)
    return (gains, filt_vars, shrinks, infos)


def e_step(looked, word_counts, topic_prior):
    counts_float = word_counts.astype(jnp.float32)
    doc_topics = topic_prior + jnp.sum(counts_float, axis=-1, keepdims=True) / K
    scores = looked.astype(jnp.float32)
    for sweep in range(EITERS):
        resp = jax.nn.softmax(lax.digamma(doc_topics)[..., None, :] + scores, axis=-1)
        doc_topics = topic_prior + jnp.sum(counts_float[..., None] * resp, axis=-2)
    weighted = (counts_float[..., None] * resp).astype(jnp.bfloat16)
    return (doc_topics, weighted)


def body(beta, word_ids, word_counts, block_slot, topic_prior, drift_var, obs_precision):
    local_beta = beta[0]
    own_words = local_beta.shape[0]
    topics = local_beta.shape[1]
    doc_devices = lax.axis_size("doc")
    doc_place = lax.axis_index("doc")
    local_peak = jnp.max(local_beta, axis=0)
    local_total = jnp.sum(jnp.exp(local_beta - local_peak), axis=0)
    slot_ids = word_ids[0]
    local_docs = slot_ids.shape[0]
    slot_width = slot_ids.shape[1]
    columns = jnp.take(block_slot, slot_ids // BLOCK) * BLOCK + slot_ids % BLOCK
    all_columns = lax.all_gather(columns, "doc", axis=0, tiled=True)
    all_counts = lax.all_gather(word_counts[0], "doc", axis=0, tiled=True)
    peaks = lax.all_gather(local_peak, "doc")
    totals = lax.all_gather(local_total, "doc")
    peak_value = jnp.max(peaks, axis=0)
    total_value = jnp.sum(totals * jnp.exp(peaks - peak_value), axis=0)
    normalizer = peak_value + jnp.log(total_value)
    flat_columns = all_columns.reshape(-1)
    local_columns = flat_columns - doc_place * own_words
    inside = (local_columns >= 0) & (local_columns < own_words)
    picked = jnp.take(local_beta, jnp.clip(local_columns, 0, own_words - 1), axis=0)
    partial = jnp.where(
        inside[:, None], (picked - normalizer).astype(jnp.bfloat16), jnp.zeros((), jnp.bfloat16)
    )
    looked = lax.psum(partial, "doc").reshape(local_docs * doc_devices, slot_width, topics)
    doc_topics_all, weighted = e_step(looked, all_counts, topic_prior)
    doc_topics = lax.dynamic_slice_in_dim(doc_topics_all, doc_place * local_docs, local_docs, 0)
    flat_weighted = weighted.reshape(-1, topics)
    row_words = lax.iota(jnp.int32, own_words)
    marks = (row_words[:, None] == local_columns[None, :]).astype(jnp.bfloat16)
    counts = jnp.dot(marks, flat_weighted, preferred_element_type=jnp.float32)
    pseudo = local_beta + jnp.log1p(counts)
    gains, filt_vars, shrinks, infos = variance_tables(obs_precision, drift_var)
    years_total = obs_precision.shape[0]
    pulls = filt_vars / (filt_vars + drift_var)
    pulls = pulls.at[-1].set(0.0)
    years = lax.axis_size("tm")
    chunk = own_words // years
    by_year = lax.all_to_all(
        pseudo.reshape(years, chunk, topics), "tm", split_axis=0, concat_axis=0, tiled=True
    )

    def filter_step(mean_prev, inputs):
        gain_now, pseudo_now = inputs
        mean_now = (1.0 - gain_now) * mean_prev + gain_now * pseudo_now
        return (mean_now, mean_now)

    zero_mean = jnp.zeros((chunk, topics), dtype=jnp.float32)
    last_mean, filtered = lax.scan(
        filter_step, zero_mean, (gains[:, None, :], by_year), unroll=True
    )

    def smooth_step(mean_next, inputs):
        pull_now, filt_now = inputs
        mean_now = pull_now * mean_next + (1.0 - pull_now) * filt_now
        return (mean_now, mean_now)

    first_mean, smoothed = lax.scan(
        smooth_step, zero_mean, (pulls[:, None, :], filtered), reverse=True, unroll=True
    )
    back = lax.all_to_all(smoothed, "tm", split_axis=0, concat_axis=0, tiled=True)
    return (back.reshape(own_words, topics)[None], doc_topics[None])


def solution(mesh):
    in_specs = (
        P("tm", "doc", None),
        P("tm", "doc", None),
        P("tm", "doc", None),
        P(),
        P(),
        P(),
        P(),
    )
    out_specs = (P("tm", "doc", None), P("tm", "doc", None))
    return jax.shard_map(body, mesh=mesh, in_specs=in_specs, out_specs=out_specs, check_vma=False)
```

profile of v0, /device:TPU:9, one launch (start us, length us, event | category | flops | bytes accessed | tf_op | source)
XLA Modules:
  0.0 144.6 jit_solution(16217126004983186146)
XLA Ops:
  7.2 1.6 %reduce_max.54 = f32[128]{0:T(128)S(1)} reduce(f32[1,2048,128]{2,1,0:T(8,128)} %param.11, f32[]{:T(128)} %constant.154.clone.1), dimensions={0,1}, to_apply=%region_3.4 | reduce | flops 262016 | bytes 1049092 | tf_op jit(solution)/shard_map/reduce_max | solution.py:55
  9.1 3.1 %all-gather.5 = f32[2,1,128]{2,1,0:T(1,128)S(1)} all-gather(f32[1,1,128]{2,1,0:T(1,128)S(1)} %bitcast.281), channel_id=4, replica_groups=mesh['tm'=16,'doc'=2] {'doc'}, dimensions={0}, use_global_device_ids=true | all-gather | bytes 1536 | tf_op jit(solution)/shard_map/all_gather | solution.py:64
  12.2 3.1 %all-gather.4 = f32[2,1,128]{2,1,0:T(1,128)S(1)} all-gather(f32[1,1,128]{2,1,0:T(1,128)S(1)} %bitcast.278), channel_id=3, replica_groups=mesh['tm'=16,'doc'=2] {'doc'}, dimensions={0}, use_global_device_ids=true | all-gather | bytes 1536 | tf_op jit(solution)/shard_map/all_gather | solution.py:63
  15.4 3.3 %gather_fusion = s32[512]{0:T(512)S(1)} fusion(s32[32]{0:T(128)S(1)} %copy-done, s32[1024]{0:T(1024)S(1)} %pad_clamp_fusion), kind=kCustom, calls=%fused_computation | custom fusion | bytes 6144 | tf_op jit(solution)/shard_map/jit(_take)/gather | solution.py:60
  18.8 3.2 %all-gather.3 = s32[2,4,128]{2,1,0:T(4,128)S(1)} all-gather(s32[1,4,128]{2,1,0:T(4,128)S(1)} %fusion.120), channel_id=1, replica_groups=mesh['tm'=16,'doc'=2] {'doc'}, dimensions={0}, use_global_device_ids=true | all-gather | bytes 6144 | tf_op jit(solution)/shard_map/all_gather | solution.py:61
  22.0 2.8 %gather_fusion.1 = f32[1024,128]{1,0:T(8,128)S(1)} fusion(f32[2048,128]{1,0:T(8,128)S(1)} %bitcast.257, s32[1024]{0:T(1024)S(1)} %broadcast_clamp_fusion), kind=kCustom, calls=%fused_computation.1 | custom fusion | bytes 1052672 | tf_op jit(solution)/shard_map/jit(_take)/gather | solution.py:71
  24.9 1.0 fusion.24
  25.9 3.2 %all-gather = s32[1,8,128]{2,0,1:T(1,128)S(1)} all-gather(s32[1,4,128]{2,0,1:T(1,128)S(1)} %bitcast.279), channel_id=2, replica_groups=mesh['tm'=16,'doc'=2] {'doc'}, dimensions={1}, use_global_device_ids=true | all-gather | bytes 6144 | tf_op jit(solution)/shard_map/all_gather | solution.py:62
  29.5 24.0 %all-reduce.2.cloned.1.call-done = bf16[1024,128]{1,0:T(8,128)(2,1)} async-done(((bf16[1024,128]{1,0:T(8,128)(2,1)}), bf16[1024,128]{1,0:T(8,128)(2,1)}) %all-reduce.2.cloned.1.call-update) | async-done | bytes 262160 | tf_op jit(solution)/shard_map/psum | solution.py:75
  53.5 1.2 fusion.6
  54.7 1.3 fusion.23
  56.1 1.4 multiply_reduce_fusion.3
  57.5 1.2 fusion.8
  61.9 2.8 %fusion.4 = f32[2048,128]{1,0:T(8,128)} fusion(bf16[1024,128]{1,0:T(8,128)(2,1)S(1)} %fusion.17, s32[1024]{0:T(1024)S(1)} %bitcast.274, f32[1,2048,128]{2,1,0:T(8,128)S(1)} %copy-done.2), kind=kOutput, calls=%fused_computation.11 | convolution fusion | flops 539230208 | bytes 2363392 | tf_op jit(solution)/shard_map/dot_general | solution.py:81
  64.7 7.0 %all-to-all-start = ((f32[16,128,128]{2,1,0:T(8,128)}), f32[16,128,128]{2,1,0:T(8,128)S(1)}, u32[]{:S(2)}, u32[]{:S(2)}) async-start(f32[16,128,128]{2,1,0:T(8,128)} %bitcast.59), calls=%async_computation | async-start | bytes 2097152 | tf_op jit(solution)/shard_map/all_to_all | solution.py:89
  71.7 12.5 %while.16 = (s32[]{:T(128)}, f32[128]{0:T(128)S(1)}, f32[16,128]{1,0:T(8,128)S(1)}, f32[16,128]{1,0:T(8,128)S(1)}, f32[16,128]{1,0:T(8,128)}, /*index=5*/f32[128]{0:T(128)S(1)}, s32[]{:T(128)}, s32[]{:T(128)}) while((s32[]{:T(128)}, f32[128]{0:T(128)S(1)}, f32[16,128]{1,0:T(8,128)S(1)}, f32[16,128]{1,0:T(8,128)S(1)}, ...), condition=%wide.region_1.0_spmd.clone, body=%wide.region_0.0_spmd.clone.sunk | while | flops 771 | bytes 5235 | solution.py:21
  71.7 0.7 fusion.137
  72.5 0.7 fusion.137
  73.3 0.7 fusion.137
  74.1 0.7 fusion.137
  74.8 0.7 fusion.137
  75.6 0.7 fusion.137
  76.4 0.7 fusion.137
  77.2 0.7 fusion.137
  78.0 0.7 fusion.137
  78.8 0.7 fusion.137
  79.5 0.7 fusion.137
  84.3 12.3 %all-to-all-done = f32[16,128,128]{2,1,0:T(8,128)S(1)} async-done(((f32[16,128,128]{2,1,0:T(8,128)}), f32[16,128,128]{2,1,0:T(8,128)S(1)}, u32[]{:S(2)}, u32[]{:S(2)}) %all-to-all-start) | async-done | bytes 1048608 | tf_op jit(solution)/shard_map/all_to_all | solution.py:89
  96.6 0.9 add_dynamic-update-slice_fusion
  107.1 4.8 %all-to-all-start.1 = ((f32[16,128,128]{2,1,0:T(8,128)}), f32[16,128,128]{2,1,0:T(8,128)S(1)}, u32[]{:S(2)}, u32[]{:S(2)}) async-start(f32[16,128,128]{2,1,0:T(8,128)} %fusion.41), calls=%async_computation.1 | async-start | bytes 2097152 | tf_op jit(solution)/shard_map/all_to_all | solution.py:111
  113.0 23.8 %all-to-all-done.1 = f32[16,128,128]{2,1,0:T(8,128)S(1)} async-done(((f32[16,128,128]{2,1,0:T(8,128)}), f32[16,128,128]{2,1,0:T(8,128)S(1)}, u32[]{:S(2)}, u32[]{:S(2)}) %all-to-all-start.1) | async-done | bytes 1048608 | tf_op jit(solution)/shard_map/all_to_all | solution.py:111
  136.8 1.0 copy.43
  (105 shorter events, 19.1 us)
Async XLA Ops:
  7.2 8.2 %copy-start = (s32[32]{0:T(128)S(1)}, s32[32]{0:T(128)}, u32[]{:S(2)}) copy-start(s32[32]{0:T(128)} %param.14) | copy-start | bytes 388
  7.2 1.7 %copy-start.2 = (f32[1,2048,128]{2,1,0:T(8,128)S(1)}, f32[1,2048,128]{2,1,0:T(8,128)}, u32[]{:S(2)}) copy-start(f32[1,2048,128]{2,1,0:T(8,128)} %param.11) | copy-start | bytes 3145732
  7.2 46.3 %all-reduce.2.cloned.1.call-start = ((), (), s32[]{:S(2)}) async-start(), calls=%async_computation.2 | async-start | bytes 524288 | tf_op jit(solution)/shard_map/psum | solution.py:75
  7.2 8.1 %copy-start.5 = (s32[1,4,128]{2,1,0:T(4,128)S(1)}, s32[1,4,128]{2,1,0:T(4,128)}, u32[]{:S(2)}) copy-start(s32[1,4,128]{2,1,0:T(4,128)} %param.12) | copy-start | bytes 6148
  24.8 1.1 copy-start.6
  24.8 4.5 %copy-start.4 = (f32[128]{0:T(128)S(1)}, f32[128]{0:T(128)}, u32[]{:S(2)}) copy-start(f32[128]{0:T(128)} %param.15) | copy-start | bytes 1540
  53.5 5.2 %copy-start.1 = (bf16[1024,128]{1,0:T(8,128)(2,1)S(1)}, bf16[1024,128]{1,0:T(8,128)(2,1)}, u32[]{:S(2)}) copy-start(bf16[1024,128]{1,0:T(8,128)(2,1)} %all-reduce.2.cloned.1.call-done) | copy-start | bytes 786436
  64.7 7.0 %copy-start.3 = (f32[128]{0:T(128)S(1)}, f32[128]{0:T(128)}, u32[]{:S(2)}) copy-start(f32[128]{0:T(128)} %param.16) | copy-start | bytes 1540
  64.7 31.9 %all-to-all-start = ((f32[16,128,128]{2,1,0:T(8,128)}), f32[16,128,128]{2,1,0:T(8,128)S(1)}, u32[]{:S(2)}, u32[]{:S(2)}) async-start(f32[16,128,128]{2,1,0:T(8,128)} %bitcast.59), calls=%async_computation | async-start | bytes 2097152 | tf_op jit(solution)/shard_map/all_to_all | solution.py:89
  107.1 29.7 %all-to-all-start.1 = ((f32[16,128,128]{2,1,0:T(8,128)}), f32[16,128,128]{2,1,0:T(8,128)S(1)}, u32[]{:S(2)}, u32[]{:S(2)}) async-start(f32[16,128,128]{2,1,0:T(8,128)} %fusion.41), calls=%async_computation.1 | async-start | bytes 2097152 | tf_op jit(solution)/shard_map/all_to_all | solution.py:111
Sparse Core Ops, SparseCore 0:
  26.0 27.4 all-reduce.1
where the time goes:
time: 146 us; the launch traced here: 145 us
  waiting for transfers between devices  60.2 us (41%)
  other arithmetic  29.6 us (20%)
  between operations  14.3 us (10%)
  local copies, waits for them, and re-layouts  13.1 us (9%)
  blocking collectives  12.6 us (9%)
  starting transfers between devices  11.8 us (8%)
  matrix products  2.76 us (2%)
    psum x1, waiting for transfers between devices, body(): lax.psum(partial, 'doc')  24 us
    all_to_all x1, waiting for transfers between devices, body(): lax.all_to_all(smoothed, 'tm', split_axis=0, concat_axis=0, tiled=True)  23.8 us
    all_to_all x1, waiting for transfers between devices, body(): lax.all_to_all(pseudo.reshape(years, chunk, topics), 'tm', split_axis=0,...  12.3 us
    add x16, other arithmetic, forward_step(): return (filt_var + drift_var, (gain_now, filt_var))  11.4 us
    all_to_all x1, starting transfers between devices, body(): lax.all_to_all(pseudo.reshape(years, chunk, topics), 'tm', split_axis=0,...  6.99 us
    unnamed x22, local copies, waits for them, and re-layouts  5.44 us
    unnamed x10, other arithmetic  5.43 us
    all_to_all x1, starting transfers between devices, body(): lax.all_to_all(smoothed, 'tm', split_axis=0, concat_axis=0, tiled=True)  4.76 us
  transfers between devices with their start and end apart: 3, of which 3 were waited for; matrix products, arithmetic and copies ran while one was open for 9% of the time, Pallas kernels for 0%

commit v1 on v0

--- a/solution.py
+++ b/solution.py
@@ -59,7 +59,32 @@
     slot_width = slot_ids.shape[1]
     columns = jnp.take(block_slot, slot_ids // BLOCK) * BLOCK + slot_ids % BLOCK
     all_columns = lax.all_gather(columns, "doc", axis=0, tiled=True)
-    all_counts = lax.all_gather(word_counts[0], "doc", axis=0, tiled=True)
+
+    def edge_edit(shard_in, chip_axis):
+        frame_out, r2, reply = (
+            lax.axis_size(chip_axis),
+            lax.axis_index(chip_axis),
+            shard_in.shape[0],
+        )
+        y_new, state_next = (shard_in, 1)
+        while state_next < frame_out:
+            y_new = jnp.concatenate(
+                [
+                    y_new,
+                    lax.ppermute(
+                        y_new,
+                        axis_name=chip_axis,
+                        perm=tuple(
+                            ((num, (num - state_next) % frame_out) for num in range(frame_out))
+                        ),
+                    ),
+                ],
+                0,
+            )
+            state_next = 2 * state_next
+        return jnp.roll(y_new, r2 * reply, 0)
+
+    all_counts = edge_edit(word_counts[0], "doc")
     peaks = lax.all_gather(local_peak, "doc")
     totals = lax.all_gather(local_total, "doc")
     peak_value = jnp.max(peaks, axis=0)

time: 146 us -> 146 us (level)
  blocking collectives: 12.6 us -> 9.36 us
  waiting for transfers between devices: 60.2 us -> 62.7 us
    all_gather x1 -> x0, blocking collectives: 3.21 us -> none  [body(): all_counts = lax.all_gather(word_counts[0], 'doc', axis=0, tiled=True)]
    psum x1, waiting for transfers between devices: 24 us -> 26.5 us  [body(): lax.psum(partial, 'doc')]
  transfers between devices with their start and end apart: 3 -> 4, of which waited for: 3 -> 3; matrix products, arithmetic and copies ran while one was open for 9% -> 16% of each run, Pallas kernels for 0% -> 0%
where the time goes in v1:
time: 146 us; the launch traced here: 145 us
  waiting for transfers between devices  62.7 us (43%)
  other arithmetic  29.5 us (20%)
  between operations  14.4 us (10%)
  local copies, waits for them, and re-layouts  13.1 us (9%)
  starting transfers between devices  13.1 us (9%)
  blocking collectives  9.36 us (6%)
  matrix products  2.76 us (2%)
    psum x1, waiting for transfers between devices, body(): lax.psum(partial, 'doc')  26.5 us
    all_to_all x1, waiting for transfers between devices, body(): lax.all_to_all(smoothed, 'tm', split_axis=0, concat_axis=0, tiled=True)  23.8 us
    all_to_all x1, waiting for transfers between devices, body(): lax.all_to_all(pseudo.reshape(years, chunk, topics), 'tm', split_axis=0,...  12.3 us
    add x16, other arithmetic, forward_step(): return (filt_var + drift_var, (gain_now, filt_var))  11.4 us
    all_to_all x1, starting transfers between devices, body(): lax.all_to_all(pseudo.reshape(years, chunk, topics), 'tm', split_axis=0,...  6.99 us
    unnamed x22, local copies, waits for them, and re-layouts  5.44 us
    unnamed x10, other arithmetic  5.43 us
    all_to_all x1, starting transfers between devices, body(): lax.all_to_all(smoothed, 'tm', split_axis=0, concat_axis=0, tiled=True)  4.76 us
  transfers between devices with their start and end apart: 4, of which 3 were waited for; matrix products, arithmetic and copies ran while one was open for 16% of the time, Pallas kernels for 0%

profile of v1, /device:TPU:9, one launch (start us, length us, event | category | flops | bytes accessed | tf_op | source)
XLA Modules:
  0.0 145.2 jit_solution(3726495791568473969)
XLA Ops:
  7.2 1.3 collective-permute-start
  8.5 1.5 %reduce_max.54 = f32[128]{0:T(128)S(1)} reduce(f32[1,2048,128]{2,1,0:T(8,128)} %param.11, f32[]{:T(128)} %constant.175.clone.1), dimensions={0,1}, to_apply=%region_3.4 | reduce | flops 262016 | bytes 1049092 | tf_op jit(solution)/shard_map/reduce_max | solution.py:55
  10.4 3.1 %all-gather.4 = f32[2,1,128]{2,1,0:T(1,128)S(1)} all-gather(f32[1,1,128]{2,1,0:T(1,128)S(1)} %bitcast.277), channel_id=3, replica_groups=mesh['tm'=16,'doc'=2] {'doc'}, dimensions={0}, use_global_device_ids=true | all-gather | bytes 1536 | tf_op jit(solution)/shard_map/all_gather | solution.py:89
  13.4 3.1 %all-gather.3 = f32[2,1,128]{2,1,0:T(1,128)S(1)} all-gather(f32[1,1,128]{2,1,0:T(1,128)S(1)} %bitcast.273), channel_id=2, replica_groups=mesh['tm'=16,'doc'=2] {'doc'}, dimensions={0}, use_global_device_ids=true | all-gather | bytes 1536 | tf_op jit(solution)/shard_map/all_gather | solution.py:88
  16.6 3.3 %gather_fusion = s32[512]{0:T(512)S(1)} fusion(s32[32]{0:T(128)S(1)} %copy-done, s32[1024]{0:T(1024)S(1)} %pad_clamp_fusion), kind=kCustom, calls=%fused_computation | custom fusion | bytes 6144 | tf_op jit(solution)/shard_map/jit(_take)/gather | solution.py:60
  20.0 3.2 %all-gather.2 = s32[2,4,128]{2,1,0:T(4,128)S(1)} all-gather(s32[1,4,128]{2,1,0:T(4,128)S(1)} %fusion.124), channel_id=1, replica_groups=mesh['tm'=16,'doc'=2] {'doc'}, dimensions={0}, use_global_device_ids=true | all-gather | bytes 6144 | tf_op jit(solution)/shard_map/all_gather | solution.py:61
  23.2 2.8 %gather_fusion.1 = f32[1024,128]{1,0:T(8,128)S(1)} fusion(f32[2048,128]{1,0:T(8,128)S(1)} %bitcast.256, s32[1024]{0:T(1024)S(1)} %broadcast_clamp_fusion), kind=kCustom, calls=%fused_computation.1 | custom fusion | bytes 1052672 | tf_op jit(solution)/shard_map/jit(_take)/gather | solution.py:96
  26.1 1.0 fusion.24
  27.5 26.5 %all-reduce.2.cloned.1.call-done = bf16[1024,128]{1,0:T(8,128)(2,1)} async-done(((bf16[1024,128]{1,0:T(8,128)(2,1)}), bf16[1024,128]{1,0:T(8,128)(2,1)}) %all-reduce.2.cloned.1.call-update) | async-done | bytes 262160 | tf_op jit(solution)/shard_map/psum | solution.py:100
  54.1 1.2 fusion.6
  55.3 1.3 fusion.23
  56.6 1.4 multiply_reduce_fusion.3
  58.1 1.2 fusion.8
  62.5 2.8 %fusion.4 = f32[2048,128]{1,0:T(8,128)} fusion(bf16[1024,128]{1,0:T(8,128)(2,1)S(1)} %fusion.17, s32[1024]{0:T(1024)S(1)} %bitcast.269, f32[1,2048,128]{2,1,0:T(8,128)S(1)} %copy-done.2), kind=kOutput, calls=%fused_computation.11 | convolution fusion | flops 539230208 | bytes 2363392 | tf_op jit(solution)/shard_map/dot_general | solution.py:106
  65.3 7.0 %all-to-all-start = ((f32[16,128,128]{2,1,0:T(8,128)}), f32[16,128,128]{2,1,0:T(8,128)S(1)}, u32[]{:S(2)}, u32[]{:S(2)}) async-start(f32[16,128,128]{2,1,0:T(8,128)} %bitcast.58), calls=%async_computation | async-start | bytes 2097152 | tf_op jit(solution)/shard_map/all_to_all | solution.py:114
  72.3 12.5 %while.16 = (s32[]{:T(128)}, f32[128]{0:T(128)S(1)}, f32[16,128]{1,0:T(8,128)S(1)}, f32[16,128]{1,0:T(8,128)S(1)}, f32[16,128]{1,0:T(8,128)}, /*index=5*/f32[128]{0:T(128)S(1)}, s32[]{:T(128)}, s32[]{:T(128)}) while((s32[]{:T(128)}, f32[128]{0:T(128)S(1)}, f32[16,128]{1,0:T(8,128)S(1)}, f32[16,128]{1,0:T(8,128)S(1)}, ...), condition=%wide.region_1.0_spmd.clone, body=%wide.region_0.0_spmd.clone.sunk | while | flops 771 | bytes 5235 | solution.py:21
  72.3 0.7 fusion.143
  73.0 0.7 fusion.143
  73.8 0.7 fusion.143
  74.6 0.7 fusion.143
  75.4 0.7 fusion.143
  76.2 0.7 fusion.143
  77.0 0.7 fusion.143
  77.7 0.7 fusion.143
  78.5 0.7 fusion.143
  79.3 0.7 fusion.143
  80.1 0.7 fusion.143
  84.9 12.3 %all-to-all-done = f32[16,128,128]{2,1,0:T(8,128)S(1)} async-done(((f32[16,128,128]{2,1,0:T(8,128)}), f32[16,128,128]{2,1,0:T(8,128)S(1)}, u32[]{:S(2)}, u32[]{:S(2)}) %all-to-all-start) | async-done | bytes 1048608 | tf_op jit(solution)/shard_map/all_to_all | solution.py:114
  97.2 0.9 add_dynamic-update-slice_fusion
  107.7 4.8 %all-to-all-start.1 = ((f32[16,128,128]{2,1,0:T(8,128)}), f32[16,128,128]{2,1,0:T(8,128)S(1)}, u32[]{:S(2)}, u32[]{:S(2)}) async-start(f32[16,128,128]{2,1,0:T(8,128)} %fusion.41), calls=%async_computation.1 | async-start | bytes 2097152 | tf_op jit(solution)/shard_map/all_to_all | solution.py:136
  113.5 23.8 %all-to-all-done.1 = f32[16,128,128]{2,1,0:T(8,128)S(1)} async-done(((f32[16,128,128]{2,1,0:T(8,128)}), f32[16,128,128]{2,1,0:T(8,128)S(1)}, u32[]{:S(2)}, u32[]{:S(2)}) %all-to-all-start.1) | async-done | bytes 1048608 | tf_op jit(solution)/shard_map/all_to_all | solution.py:136
  137.4 1.0 copy.42
  (105 shorter events, 19.1 us)
Async XLA Ops:
  7.2 9.4 %copy-start = (s32[32]{0:T(128)S(1)}, s32[32]{0:T(128)}, u32[]{:S(2)}) copy-start(s32[32]{0:T(128)} %param.14) | copy-start | bytes 388
  7.2 2.9 %copy-start.2 = (f32[1,2048,128]{2,1,0:T(8,128)S(1)}, f32[1,2048,128]{2,1,0:T(8,128)}, u32[]{:S(2)}) copy-start(f32[1,2048,128]{2,1,0:T(8,128)} %param.11) | copy-start | bytes 3145732
  7.2 46.9 %all-reduce.2.cloned.1.call-start = ((), (), s32[]{:S(2)}) async-start(), calls=%async_computation.2 | async-start | bytes 524288 | tf_op jit(solution)/shard_map/psum | solution.py:100
  7.2 20.0 %collective-permute-start = (s32[4,128]{1,0:T(4,128)}, s32[4,128]{1,0:T(4,128)S(1)}, u32[]{:S(2)}, u32[]{:S(2)}) collective-permute-start(s32[4,128]{1,0:T(4,128)} %bitcast.274), channel_id=1, source_target_pairs={{0,1},{1,0},{2,3},{3,2},{4,5},{5,4},{6,7},{7,6},{8,9},{9,8},{10,11... | collective-permute-start | bytes 6152 | tf_op jit(solution)/shard_map/ppermute | solution.py:74
  8.5 8.0 %copy-start.5 = (s32[1,4,128]{2,1,0:T(4,128)S(1)}, s32[1,4,128]{2,1,0:T(4,128)}, u32[]{:S(2)}) copy-start(s32[1,4,128]{2,1,0:T(4,128)} %param.12) | copy-start | bytes 6148
  26.1 1.2 copy-start.6
  26.1 1.3 copy-start.4
  54.1 5.2 %copy-start.1 = (bf16[1024,128]{1,0:T(8,128)(2,1)S(1)}, bf16[1024,128]{1,0:T(8,128)(2,1)}, u32[]{:S(2)}) copy-start(bf16[1024,128]{1,0:T(8,128)(2,1)} %all-reduce.2.cloned.1.call-done) | copy-start | bytes 786436
  65.3 7.0 %copy-start.3 = (f32[128]{0:T(128)S(1)}, f32[128]{0:T(128)}, u32[]{:S(2)}) copy-start(f32[128]{0:T(128)} %param.16) | copy-start | bytes 1540
  65.3 31.9 %all-to-all-start = ((f32[16,128,128]{2,1,0:T(8,128)}), f32[16,128,128]{2,1,0:T(8,128)S(1)}, u32[]{:S(2)}, u32[]{:S(2)}) async-start(f32[16,128,128]{2,1,0:T(8,128)} %bitcast.58), calls=%async_computation | async-start | bytes 2097152 | tf_op jit(solution)/shard_map/all_to_all | solution.py:114
  107.7 29.7 %all-to-all-start.1 = ((f32[16,128,128]{2,1,0:T(8,128)}), f32[16,128,128]{2,1,0:T(8,128)S(1)}, u32[]{:S(2)}, u32[]{:S(2)}) async-start(f32[16,128,128]{2,1,0:T(8,128)} %fusion.41), calls=%async_computation.1 | async-start | bytes 2097152 | tf_op jit(solution)/shard_map/all_to_all | solution.py:136
Sparse Core Ops, SparseCore 0:
  27.3 26.7 all-reduce.1
